TPU v7x, 512 devices: a whole 4x4x16 slice. The times are simulated.
512 devices in a mesh: req: 128 (over x, z, core), mlp: 4 (over y).
Axes of the slice: x: 4, y: 4, z: 16, core: 2. Of those that a mesh axis runs over, the one named last changes fastest.
Arguments:
- queries: bfloat16 [32768, 8, 256], P('req', 'mlp'), may hold values from -7 to 7
- new_kv: bfloat16 [32768, 8, 512], P('req', 'mlp'), may hold values from -6 to 6
- cache_pool: bfloat16 [768, 128, 8, 512], P('req', None, 'mlp'), may hold values from -6 to 6
- page_table: int32 [128, 6], P('req'), may hold values from 0 to 5, each once within a row
- assignment: int32 [128], P('req'), may hold values from 0 to 127, each once
- lengths: int32 [128], replicated, may hold values from 1 to 768, 24576 in all
- lambda_vectors: float32 [4, 128], replicated, may hold values from -0.4 to 0.4
- subln_gain: float32 [256], replicated, may hold values from 0.5 to 1.5
- residual: bfloat16 [32768, 2048], P('req', 'mlp'), may hold values from -70 to 70
- out_weight: bfloat16 [2048, 2048], P('req', 'mlp'), may hold values from -0.125 to 0.125
- norm_gain: float32 [2048], replicated, may hold values from 0.5 to 1.5
- gate_weight: bfloat16 [2048, 3072], P('req', 'mlp'), may hold values from -0.125 to 0.125
- up_weight: bfloat16 [2048, 3072], P('req', 'mlp'), may hold values from -0.125 to 0.125
- down_weight_t: bfloat16 [2048, 3072], P('req', 'mlp'), may hold values from -0.109375 to 0.109375
Outputs:
- layer_out: bfloat16 [32768, 2048], P('req', 'mlp')
Inputs may be any that keep to these rules, and one draw needn't show every extreme that they name: `page_table`: row g lists the cache pages of slot g in logical order as offsets from page g * 6; each offset once in a row. `assignment`: every request is served by exactly one slot. `lengths`: indexed by request; some request has exactly 768 cached tokens.
All inputs are finite; a program needn't handle non-finite values.
Results may differ from a plain program's by a relative error of at most 0.011.
Values may be sent and summed in bfloat16 or wider, within the bound.
No kernel may reach another device: no remote copies, remote signals or barrier semaphores. Data moves between devices by JAX's collectives and lax.ppermute only.
A program may use at most 64 MiB of HBM per device.

v0:
```python
import jax
import jax.numpy as jnp
from jax import lax
from jax.sharding import Mesh, PartitionSpec as P

D = 2048
NEG_FILL = -1e30
LAMBDA_BASE = 0.2


def attend(
    queries, new_kv, cache_pool, page_table, assignment, lengths, lambda_vectors, subln_gain
):
    row_count, head_count, value_width = queries.shape
    half_size = value_width // 2
    score_scale = half_size ** (-0.5)
    request = assignment[0]
    cached = jnp.sum(
        jnp.where(jnp.arange(lengths.shape[0], dtype=jnp.int32) == request, lengths, 0)
    )
    pages = jnp.take(cache_pool, page_table[0], axis=0)
    cached_rows = pages.reshape(-1, head_count, cache_pool.shape[3])
    cache_len = cached_rows.shape[0]
    key_rows = jnp.concatenate([cached_rows, new_kv], axis=0)
    positions = jnp.arange(cache_len, dtype=jnp.int32)
    token_pos = jnp.arange(row_count, dtype=jnp.int32)
    visible = jnp.concatenate(
        [
            jnp.broadcast_to((positions < cached)[None, :], (row_count, cache_len)),
            token_pos[None, :] <= token_pos[:, None],
        ],
        axis=1,
    )
    value_rows = key_rows[:, :, 2 * half_size :]

    def one_map(query_rows, key_half):
        score = (
            jnp.einsum("nhd,khd->nhk", query_rows, key_half, preferred_element_type=jnp.float32)
            * score_scale
        )
        score = jnp.where(visible[:, None, :], score, NEG_FILL)
        row_max = jnp.max(score, axis=2, keepdims=True)
        exp_terms = jnp.where(visible[:, None, :], jnp.exp(score - row_max), 0.0)
        exp_total = jnp.sum(exp_terms, axis=2)
        mixed = jnp.einsum(
            "nhk,khd->nhd",
            exp_terms.astype(jnp.bfloat16),
            value_rows,
            preferred_element_type=jnp.float32,
        )
        return mixed / exp_total[:, :, None]

    map_one = one_map(queries[:, :, :half_size], key_rows[:, :, :half_size])
    map_two = one_map(queries[:, :, half_size:], key_rows[:, :, half_size : 2 * half_size])
    lambda_now = (
        jnp.exp(jnp.sum(lambda_vectors[0] * lambda_vectors[1]))
        - jnp.exp(jnp.sum(lambda_vectors[2] * lambda_vectors[3]))
        + LAMBDA_BASE
    )
    mix_out = map_one - lambda_now * map_two
    mix_out = (
        mix_out
        * lax.rsqrt(jnp.mean(mix_out * mix_out, axis=2, keepdims=True) + 1e-05)
        * subln_gain
        * (1.0 - LAMBDA_BASE)
    )
    return mix_out.astype(jnp.bfloat16).reshape(row_count, head_count * value_width)


def mlp_gather(block, axis_size):
    index = lax.axis_index("mlp")
    pieces = [block]
    for shift in range(1, axis_size):
        pieces.append(
            lax.ppermute(block, "mlp", [(i, (i + shift) % axis_size) for i in range(axis_size)])
        )
    stacked = jnp.stack(pieces, axis=0)
    source_of = (index - jnp.arange(axis_size, dtype=jnp.int32)) % axis_size
    gathered = jnp.take(stacked, source_of, axis=0)
    return jnp.concatenate([gathered[k] for k in range(axis_size)], axis=1)


def down_and_scatter(hidden_act, down_halves, axis_size, rows):
    index = lax.axis_index("mlp")
    nx, nz, nc = [lax.axis_size(name) for name in REQ_PARTS]
    n = hidden_act.shape[0]
    own = lax.axis_index("c")
    parts = []
    for half in down_halves:
        value = lax.dot_general(
            hidden_act, half, (((1,), (1,)), ((), ())), preferred_element_type=jnp.float32
        )
        parts.append(value.astype(jnp.bfloat16).reshape(n, nz, nx, rows))

    def block_for(target):
        picks = [lax.dynamic_index_in_dim(p, target, 2, keepdims=False) for p in parts]
        first = jnp.where(own == 0, picks[0], picks[1])
        second = jnp.where(own == 0, picks[1], picks[0])
        return jnp.stack([first, second], axis=2).reshape(n, -1)

    incoming = []
    for shift in range(1, axis_size):
        target = (index + shift) % axis_size
        incoming.append(
            lax.ppermute(
                block_for(target), "mlp", [(i, (i + shift) % axis_size) for i in range(axis_size)]
            )
        )
    total = block_for(index).astype(jnp.float32)
    for received in incoming:
        total = total + received.astype(jnp.float32)
    return total


REQ_PARTS = ("x", "z", "c")


def gather_over_xz(block):
    out = lax.all_gather(block, "x", axis=0, tiled=True)
    return lax.all_gather(out, "z", axis=0, tiled=True)


def swap_with_core(rows_xz):
    return [rows_xz, lax.ppermute(rows_xz, "c", [(0, 1), (1, 0)])]


def split_dot(act, halves):
    size = halves[0].shape[0]
    total = None
    for j, half in enumerate(halves):
        part = jnp.dot(act[:, j * size : (j + 1) * size], half, preferred_element_type=jnp.float32)
        total = part if total is None else total + part
    return total


def to_gathered_order(act, rows):
    nx, nz, nc = [lax.axis_size(name) for name in REQ_PARTS]
    n = act.shape[0]
    own = lax.axis_index("c")
    split = act.reshape(n, nx, nz, nc, rows)
    split = jnp.where(own == 0, split, split[:, :, :, ::-1, :])
    return split.transpose(0, 3, 2, 1, 4).reshape(n, -1)


def per_device(
    queries,
    new_kv,
    cache_pool,
    page_table,
    assignment,
    lengths,
    lambda_vectors,
    subln_gain,
    residual,
    out_weight,
    norm_gain,
    gate_weight,
    up_weight,
    down_weight_t,
):
    widths = [out_weight.shape[1], gate_weight.shape[1], up_weight.shape[1], down_weight_t.shape[1]]
    packed = jnp.concatenate([out_weight, gate_weight, up_weight, down_weight_t], axis=1)
    rows_xz = gather_over_xz(packed)
    attn_out = attend(
        queries, new_kv, cache_pool, page_table, assignment, lengths, lambda_vectors, subln_gain
    )
    mlp_size = D // residual.shape[1]
    heads_all = mlp_gather(attn_out, mlp_size)
    rows_xz, heads_all = lax.optimization_barrier((rows_xz, heads_all))
    halves = swap_with_core(rows_xz)
    bounds = [0]
    for w in widths:
        bounds.append(bounds[-1] + w)
    out_full, gate_full, up_full, down_full = [
        [half[:, bounds[i] : bounds[i + 1]] for half in halves] for i in range(4)
    ]
    rows = out_weight.shape[0]
    projected = split_dot(to_gathered_order(heads_all, rows), out_full)
    stream = (residual.astype(jnp.float32) + projected).astype(jnp.bfloat16)
    stream_all = mlp_gather(stream, mlp_size).astype(jnp.float32)
    squares = jnp.sum(stream_all * stream_all, axis=1, keepdims=True)
    normed = (stream_all * lax.rsqrt(squares / D + 1e-05) * norm_gain).astype(jnp.bfloat16)
    normed = to_gathered_order(normed, rows)
    gate_up = split_dot(normed, [half[:, bounds[1] : bounds[3]] for half in halves])
    gate_value = gate_up[:, : widths[1]]
    up_value = gate_up[:, widths[1] :]
    hidden_act = (jax.nn.silu(gate_value) * up_value).astype(jnp.bfloat16)
    summed = down_and_scatter(hidden_act, down_full, mlp_size, out_weight.shape[0])
    return (stream.astype(jnp.float32) + summed).astype(jnp.bfloat16)


def solution(mesh):
    split = Mesh(mesh.devices.reshape(4, 16, 2, mesh.devices.shape[1]), REQ_PARTS + ("mlp",))
    req = REQ_PARTS
    in_specs = (
        P(req, "mlp", None),
        P(req, "mlp", None),
        P(req, None, "mlp", None),
        P(req, None),
        P(req),
        P(),
        P(),
        P(),
        P(req, "mlp"),
        P(req, "mlp"),
        P(),
        P(req, "mlp"),
        P(req, "mlp"),
        P(req, "mlp"),
    )
    out_specs = P(req, "mlp")
    return jax.shard_map(
        per_device, mesh=split, in_specs=in_specs, out_specs=out_specs, check_vma=False
    )
```

profile of v0, /device:TPU:13, one launch (start us, length us, event | category | flops | bytes accessed | tf_op | source)
XLA Modules:
  0.0 189.5 jit_solution(5457327461825373114)
XLA Ops:
  6.5 0.9 pad_maximum_fusion.19
  7.4 9.8 %all_gather.6 = bf16[64,2816]{1,0:T(8,128)(2,1)} all-gather(bf16[16,2816]{1,0:T(8,128)(2,1)S(1)} %pad_maximum_fusion.19), channel_id=1, replica_groups=mesh['x'=4,'z'=16,'c'=2,'mlp'=4] {'x'}, dimensions={0}, use_global_device_ids=true | all-gather | bytes 450560 | tf_op jit(solution)/shard_map/all_gather | solution.py:119
  17.9 5.6 %gather_fusion = bf16[6,128,2,512]{3,2,1,0:T(2,128)(2,1)} fusion(bf16[6,128,2,512]{3,2,1,0:T(2,128)(2,1)S(1)} %copy-done, s32[1024]{0:T(1024)S(1)} %pad_clamp_fusion.1), kind=kCustom, calls=%fused_computation.2 | custom fusion | bytes 3145752 | tf_op jit(solution)/shard_map/jit(_take)/gather | solution.py:21
  23.5 1.7 copy.47
  25.3 0.8 copy.48
  26.8 0.7 multiply_reduce_fusion.2
  28.8 0.7 fusion.79
  29.5 0.7 iota_compare_fusion.1
  30.6 1.8 fusion.110
  32.4 1.5 bitcast_select_fusion.4
  33.9 2.3 %fusion.111 = f32[256,2]{0,1:T(2,128)S(1)} fusion(pred[256,1024]{0,1:T(8,128)(4,1)S(1)} %pad_add_fusion, bf16[768,2,512]{2,0,1:T(8,128)(2,1)} %bitcast_select_fusion.4, bf16[256,2,512]{2,0,1:T(8,128)(2,1)} %copy.48, bf16[256,2,128]{2,1,0:T(2,128)(2,1)} %get-tuple-element.33), kind=kOutput, calls=%fused_computation.142 | convolution fusion | flops 137888768 | bytes 2754560 | tf_op jit(solution)/shard_map/sub | solution.py:43
  36.2 3.2 %fusion.21 = f32[256,2,256]{0,2,1:T(8,128)} fusion(f32[256,2]{0,1:T(2,128)S(1)} %fusion.111, pred[256,1024]{0,1:T(8,128)(4,1)S(1)} %pad_add_fusion, bf16[768,2,512]{2,0,1:T(8,128)(2,1)S(1)} %copy-done.1, bf16[256,2,512]{2,0,1:T(8,128)(2,1)} %copy.48, bf16[256,2,128]{2,1,0:T(2,128)(2,1)} %get-tuple-element.33), kind=kOutput, calls=%fused_computation.34 | convolution fusion | flops 408552960 | bytes 5376000 | tf_op jit(solution)/shard_map/nhk,khd->nhd/dot_general | solution.py:45
  39.4 2.0 %fusion.116 = f32[256,2]{0,1:T(2,128)S(1)} fusion(pred[256,1024]{0,1:T(8,128)(4,1)S(1)} %pad_add_fusion, bf16[256,2,512]{2,0,1:T(8,128)(2,1)} %copy.48, bf16[768,2,512]{2,0,1:T(8,128)(2,1)S(1)} %copy-done.1, bf16[256,2,128]{2,1,0:T(2,128)(2,1)S(1)} %get-tuple-element.32), kind=kOutput, calls=%fused_computation.143 | convolution fusion | flops 137888768 | bytes 2492416 | tf_op jit(solution)/shard_map/sub | solution.py:43
  41.4 3.5 %multiply_reduce_fusion.1 = (f32[256,2]{0,1:T(2,128)S(1)}, f32[256,2,256]{0,2,1:T(8,128)}) fusion(f32[256,2,256]{0,2,1:T(8,128)} %fusion.21, f32[256,2]{0,1:T(2,128)S(1)} %fusion.116, pred[256,1024]{0,1:T(8,128)(4,1)S(1)} %pad_add_fusion, bf16[256,2,512]{2,0,1:T(8,128)(2,1)} %copy.48, bf16[768,2,512]{2,0,1:T(8,128)(2,1)S(1)} %copy-done.1, ...), kind=kOutput, calls=%fused_computation.73 | convolution fusion | flops 409076736 | bytes 5902340 | tf_op jit(solution)/shard_map/nhk,khd->nhd/dot_general | solution.py:45
  44.9 1.2 multiply_convert_fusion.1
  46.0 3.2 %collective-permute-start = (bf16[256,512]{0,1:T(8,128)(2,1)S(1)}, bf16[256,512]{0,1:T(8,128)(2,1)S(1)}, u32[]{:S(2)}, u32[]{:S(2)}) collective-permute-start(bf16[256,512]{0,1:T(8,128)(2,1)S(1)} %bitcast.105), channel_id=1, source_target_pairs={{0,1},{1,2},{2,3},{3,0},{4,5},{5,6},{6,7},{7,4},{8,9},{9,10},{10,1... | collective-permute-start | bytes 786440 | tf_op jit(solution)/shard_map/ppermute | solution.py:75
  49.2 2.6 %collective-permute-start.1 = (bf16[256,512]{0,1:T(8,128)(2,1)S(1)}, bf16[256,512]{0,1:T(8,128)(2,1)S(1)}, u32[]{:S(2)}, u32[]{:S(2)}) collective-permute-start(bf16[256,512]{0,1:T(8,128)(2,1)S(1)} %bitcast.106), channel_id=1, source_target_pairs={{0,2},{1,3},{2,0},{3,1},{4,6},{5,7},{6,4},{7,5},{8,10},{9,11},{10,... | collective-permute-start | bytes 786440 | tf_op jit(solution)/shard_map/ppermute | solution.py:75
  51.8 4.0 %collective-permute-start.2 = (bf16[256,512]{0,1:T(8,128)(2,1)S(1)}, bf16[256,512]{0,1:T(8,128)(2,1)S(1)}, u32[]{:S(2)}, u32[]{:S(2)}) collective-permute-start(bf16[256,512]{0,1:T(8,128)(2,1)S(1)} %bitcast.107), channel_id=1, source_target_pairs={{0,3},{1,0},{2,1},{3,2},{4,7},{5,4},{6,5},{7,6},{8,11},{9,8},{10,9... | collective-permute-start | bytes 786440 | tf_op jit(solution)/shard_map/ppermute | solution.py:75
  55.9 2.4 %collective-permute-done.1 = bf16[256,512]{0,1:T(8,128)(2,1)S(1)} collective-permute-done((bf16[256,512]{0,1:T(8,128)(2,1)S(1)}, bf16[256,512]{0,1:T(8,128)(2,1)S(1)}, u32[]{:S(2)}, u32[]{:S(2)}) %collective-permute-start.1) | collective-permute-done | bytes 262176 | tf_op jit(solution)/shard_map/ppermute | solution.py:75
  58.3 2.8 %collective-permute-done.2 = bf16[256,512]{0,1:T(8,128)(2,1)S(1)} collective-permute-done((bf16[256,512]{0,1:T(8,128)(2,1)S(1)}, bf16[256,512]{0,1:T(8,128)(2,1)S(1)}, u32[]{:S(2)}, u32[]{:S(2)}) %collective-permute-start.2) | collective-permute-done | bytes 262176 | tf_op jit(solution)/shard_map/ppermute | solution.py:75
  61.0 1.1 pad_maximum_fusion
  62.2 1.9 gather_fusion.1
  64.4 39.7 %all-gather.2.cloned.1.call-done = bf16[1024,2816]{1,0:T(8,128)(2,1)} async-done(((bf16[64,2816]{1,0:T(8,128)(2,1)}), bf16[1024,2816]{1,0:T(8,128)(2,1)}) %all-gather.2.cloned.1.call-update) | async-done | bytes 5767184 | tf_op jit(solution)/shard_map/all_gather | solution.py:120
  104.0 7.7 %collective-permute-start.3 = (bf16[1024,2816]{1,0:T(8,128)(2,1)}, bf16[1024,2816]{1,0:T(8,128)(2,1)}, u32[]{:S(2)}, u32[]{:S(2)}) collective-permute-start(bf16[1024,2816]{1,0:T(8,128)(2,1)} %all-gather.2.cloned.1.call-done), channel_id=1, source_target_pairs={{0,4},{4,0},{1,5},{5,1},{2,6},{6,2},{3,7},{7,3},{8,12},{12,8},{9,1... | collective-permute-start | bytes 17301512 | tf_op jit(solution)/shard_map/ppermute | solution.py:124
  112.4 1.7 fusion.31
  114.1 7.0 %collective-permute-done.3 = bf16[1024,2816]{1,0:T(8,128)(2,1)} collective-permute-done((bf16[1024,2816]{1,0:T(8,128)(2,1)}, bf16[1024,2816]{1,0:T(8,128)(2,1)}, u32[]{:S(2)}, u32[]{:S(2)}) %collective-permute-start.3) | collective-permute-done | bytes 5767200 | tf_op jit(solution)/shard_map/ppermute | solution.py:124
  121.1 1.7 fusion.26
  122.8 3.1 %collective-permute-start.4 = (bf16[256,512]{1,0:T(8,128)(2,1)S(1)}, bf16[256,512]{1,0:T(8,128)(2,1)S(1)}, u32[]{:S(2)}, u32[]{:S(2)}) collective-permute-start(bf16[256,512]{1,0:T(8,128)(2,1)S(1)} %fusion.26), channel_id=1, source_target_pairs={{0,1},{1,2},{2,3},{3,0},{4,5},{5,6},{6,7},{7,4},{8,9},{9,10},{10,1... | collective-permute-start | bytes 786440 | tf_op jit(solution)/shard_map/ppermute | solution.py:75
  125.9 2.6 %collective-permute-start.5 = (bf16[256,512]{1,0:T(8,128)(2,1)S(1)}, bf16[256,512]{1,0:T(8,128)(2,1)S(1)}, u32[]{:S(2)}, u32[]{:S(2)}) collective-permute-start(bf16[256,512]{1,0:T(8,128)(2,1)S(1)} %fusion.26), channel_id=1, source_target_pairs={{0,2},{1,3},{2,0},{3,1},{4,6},{5,7},{6,4},{7,5},{8,10},{9,11},{10,... | collective-permute-start | bytes 786440 | tf_op jit(solution)/shard_map/ppermute | solution.py:75
  128.5 4.1 %collective-permute-start.6 = (bf16[256,512]{1,0:T(8,128)(2,1)S(1)}, bf16[256,512]{1,0:T(8,128)(2,1)S(1)}, u32[]{:S(2)}, u32[]{:S(2)}) collective-permute-start(bf16[256,512]{1,0:T(8,128)(2,1)S(1)} %fusion.26), channel_id=1, source_target_pairs={{0,3},{1,0},{2,1},{3,2},{4,7},{5,4},{6,5},{7,6},{8,11},{9,8},{10,9... | collective-permute-start | bytes 786440 | tf_op jit(solution)/shard_map/ppermute | solution.py:75
  132.8 3.8 %collective-permute-done.5 = bf16[256,512]{1,0:T(8,128)(2,1)S(1)} collective-permute-done((bf16[256,512]{1,0:T(8,128)(2,1)S(1)}, bf16[256,512]{1,0:T(8,128)(2,1)S(1)}, u32[]{:S(2)}, u32[]{:S(2)}) %collective-permute-start.5) | collective-permute-done | bytes 262176 | tf_op jit(solution)/shard_map/ppermute | solution.py:75
  136.5 6.6 %collective-permute-done.6 = bf16[256,512]{1,0:T(8,128)(2,1)S(1)} collective-permute-done((bf16[256,512]{1,0:T(8,128)(2,1)S(1)}, bf16[256,512]{1,0:T(8,128)(2,1)S(1)}, u32[]{:S(2)}, u32[]{:S(2)}) %collective-permute-start.6) | collective-permute-done | bytes 262176 | tf_op jit(solution)/shard_map/ppermute | solution.py:75
  143.1 1.1 pad_maximum_fusion.2
  144.3 1.8 gather_fusion.2
  148.2 2.9 %fusion.4 = f32[256,1536]{1,0:T(8,128)S(1)} fusion(bf16[1024,2816]{1,0:T(8,128)(2,1)} %all-gather.2.cloned.1.call-done, bf16[256,2048]{0,1:T(8,128)(2,1)S(1)} %bitcast.95), kind=kOutput, calls=%fused_computation.7 | convolution fusion | flops 805306368 | bytes 5242880 | tf_op jit(solution)/shard_map/dot_general | solution.py:131
  151.1 2.9 %fusion.6 = f32[256,1536]{1,0:T(8,128)S(1)} fusion(f32[256,1536]{1,0:T(8,128)S(1)} %fusion.4, bf16[1024,2816]{1,0:T(8,128)(2,1)} %collective-permute-done.3, bf16[256,2048]{0,1:T(8,128)(2,1)S(1)} %bitcast.96), kind=kOutput, calls=%fused_computation.9 | convolution fusion | flops 805699584 | bytes 6815744 | tf_op jit(solution)/shard_map/dot_general | solution.py:131
  154.3 0.7 copy-done.3
  155.0 2.0 %fusion.15 = bf16[256,1024]{1,0:T(8,128)(2,1)S(1)} fusion(bf16[256,768]{1,0:T(8,128)(2,1)S(1)} %fusion.41, bf16[1024,2816]{1,0:T(8,128)(2,1)} %all-gather.2.cloned.1.call-done), kind=kOutput, calls=%fused_computation.29 | convolution fusion | flops 402915328 | bytes 2490368 | tf_op jit(solution)/shard_map/dot_general | solution.py:90
  157.2 2.1 %fusion.18 = bf16[256,1024]{1,0:T(8,128)(2,1)S(1)} fusion(bf16[256,768]{1,0:T(8,128)(2,1)} %copy-done.3, bf16[1024,2816]{1,0:T(8,128)(2,1)} %collective-permute-done.3), kind=kOutput, calls=%fused_computation.30 | convolution fusion | flops 402915328 | bytes 2490368 | tf_op jit(solution)/shard_map/dot_general | solution.py:90
  159.7 0.8 copy.63
  160.6 1.9 %collective-permute-start.7 = (bf16[256,512]{1,0:T(8,128)(2,1)}, bf16[256,512]{1,0:T(8,128)(2,1)}, u32[]{:S(2)}, u32[]{:S(2)}) collective-permute-start(bf16[256,512]{1,0:T(8,128)(2,1)} %copy.63), channel_id=1, source_target_pairs={{0,1},{1,2},{2,3},{3,0},{4,5},{5,6},{6,7},{7,4},{8,9},{9,10},{10,1... | collective-permute-start | bytes 786440 | tf_op jit(solution)/shard_map/ppermute | solution.py:105
  162.6 0.8 copy.65
  163.4 2.2 %collective-permute-start.8 = (bf16[256,512]{1,0:T(8,128)(2,1)}, bf16[256,512]{1,0:T(8,128)(2,1)S(1)}, u32[]{:S(2)}, u32[]{:S(2)}) collective-permute-start(bf16[256,512]{1,0:T(8,128)(2,1)} %copy.65), channel_id=1, source_target_pairs={{0,2},{1,3},{2,0},{3,1},{4,6},{5,7},{6,4},{7,5},{8,10},{9,11},{10,... | collective-permute-start | bytes 786440 | tf_op jit(solution)/shard_map/ppermute | solution.py:105
  165.6 0.8 copy.66
  166.4 4.0 %collective-permute-start.9 = (bf16[256,512]{1,0:T(8,128)(2,1)}, bf16[256,512]{1,0:T(8,128)(2,1)S(1)}, u32[]{:S(2)}, u32[]{:S(2)}) collective-permute-start(bf16[256,512]{1,0:T(8,128)(2,1)} %copy.66), channel_id=1, source_target_pairs={{0,3},{1,0},{2,1},{3,2},{4,7},{5,4},{6,5},{7,6},{8,11},{9,8},{10,9... | collective-permute-start | bytes 786440 | tf_op jit(solution)/shard_map/ppermute | solution.py:105
  170.7 3.0 %collective-permute-done.8 = bf16[256,512]{1,0:T(8,128)(2,1)S(1)} collective-permute-done((bf16[256,512]{1,0:T(8,128)(2,1)}, bf16[256,512]{1,0:T(8,128)(2,1)S(1)}, u32[]{:S(2)}, u32[]{:S(2)}) %collective-permute-start.8) | collective-permute-done | bytes 262176 | tf_op jit(solution)/shard_map/ppermute | solution.py:105
  173.7 7.1 %collective-permute-done.9 = bf16[256,512]{1,0:T(8,128)(2,1)S(1)} collective-permute-done((bf16[256,512]{1,0:T(8,128)(2,1)}, bf16[256,512]{1,0:T(8,128)(2,1)S(1)}, u32[]{:S(2)}, u32[]{:S(2)}) %collective-permute-start.9) | collective-permute-done | bytes 262176 | tf_op jit(solution)/shard_map/ppermute | solution.py:105
  180.8 1.8 add_convert_fusion
  (60 shorter events, 5.2 us)
Async XLA Ops:
  6.5 11.4 %copy-start = (bf16[6,128,2,512]{3,2,1,0:T(2,128)(2,1)S(1)}, bf16[6,128,2,512]{3,2,1,0:T(2,128)(2,1)}, u32[]{:S(2)}) copy-start(bf16[6,128,2,512]{3,2,1,0:T(2,128)(2,1)} %param.18) | copy-start | bytes 4718596
  6.5 97.5 %all-gather.2.cloned.1.call-start = ((), (), s32[]{:S(2)}) async-start(), calls=%async_computation | async-start | bytes 6127616 | tf_op jit(solution)/shard_map/all_gather | solution.py:120
  23.5 1.8 copy-start.2
  23.5 3.3 %copy-start.5 = (f32[4,128]{1,0:T(4,128)S(1)}, f32[4,128]{1,0:T(4,128)}, u32[]{:S(2)}) copy-start(f32[4,128]{1,0:T(4,128)} %param.22) | copy-start | bytes 6148
  23.5 5.3 %copy-start.8 = (s32[128]{0:T(128)S(1)}, s32[128]{0:T(128)}, u32[]{:S(2)}) copy-start(s32[128]{0:T(128)} %param.21) | copy-start | bytes 1540
  23.5 6.8 %copy-start.9 = (s32[1,6]{1,0:T(1,128)S(1)}, s32[1,6]{1,0:T(1,128)}, u32[]{:S(2)}) copy-start(s32[1,6]{1,0:T(1,128)} %param.19) | copy-start | bytes 76
  33.9 2.3 %copy-start.1 = (bf16[768,2,512]{2,0,1:T(8,128)(2,1)S(1)}, bf16[768,2,512]{2,0,1:T(8,128)(2,1)}, u32[]{:S(2)}) copy-start(bf16[768,2,512]{2,0,1:T(8,128)(2,1)} %bitcast_select_fusion.4) | copy-start | bytes 4718596
  41.4 3.5 %copy-start.6 = (f32[256]{0:T(256)S(1)}, f32[256]{0:T(256)}, u32[]{:S(2)}) copy-start(f32[256]{0:T(256)} %param.23) | copy-start | bytes 3076
  46.0 9.8 %collective-permute-start = (bf16[256,512]{0,1:T(8,128)(2,1)S(1)}, bf16[256,512]{0,1:T(8,128)(2,1)S(1)}, u32[]{:S(2)}, u32[]{:S(2)}) collective-permute-start(bf16[256,512]{0,1:T(8,128)(2,1)S(1)} %bitcast.105), channel_id=1, source_target_pairs={{0,1},{1,2},{2,3},{3,0},{4,5},{5,6},{6,7},{7,4},{8,9},{9,10},{10,1... | collective-permute-start | bytes 786440 | tf_op jit(solution)/shard_map/ppermute | solution.py:75
  49.2 9.0 %collective-permute-start.1 = (bf16[256,512]{0,1:T(8,128)(2,1)S(1)}, bf16[256,512]{0,1:T(8,128)(2,1)S(1)}, u32[]{:S(2)}, u32[]{:S(2)}) collective-permute-start(bf16[256,512]{0,1:T(8,128)(2,1)S(1)} %bitcast.106), channel_id=1, source_target_pairs={{0,2},{1,3},{2,0},{3,1},{4,6},{5,7},{6,4},{7,5},{8,10},{9,11},{10,... | collective-permute-start | bytes 786440 | tf_op jit(solution)/shard_map/ppermute | solution.py:75
  51.8 9.2 %collective-permute-start.2 = (bf16[256,512]{0,1:T(8,128)(2,1)S(1)}, bf16[256,512]{0,1:T(8,128)(2,1)S(1)}, u32[]{:S(2)}, u32[]{:S(2)}) collective-permute-start(bf16[256,512]{0,1:T(8,128)(2,1)S(1)} %bitcast.107), channel_id=1, source_target_pairs={{0,3},{1,0},{2,1},{3,2},{4,7},{5,4},{6,5},{7,6},{8,11},{9,8},{10,9... | collective-permute-start | bytes 786440 | tf_op jit(solution)/shard_map/ppermute | solution.py:75
  104.0 17.1 %collective-permute-start.3 = (bf16[1024,2816]{1,0:T(8,128)(2,1)}, bf16[1024,2816]{1,0:T(8,128)(2,1)}, u32[]{:S(2)}, u32[]{:S(2)}) collective-permute-start(bf16[1024,2816]{1,0:T(8,128)(2,1)} %all-gather.2.cloned.1.call-done), channel_id=1, source_target_pairs={{0,4},{4,0},{1,5},{5,1},{2,6},{6,2},{3,7},{7,3},{8,12},{12,8},{9,1... | collective-permute-start | bytes 17301512 | tf_op jit(solution)/shard_map/ppermute | solution.py:124
  112.2 8.9 %copy-start.7 = (bf16[256,512]{1,0:T(8,128)(2,1)S(1)}, bf16[256,512]{1,0:T(8,128)(2,1)}, u32[]{:S(2)}) copy-start(bf16[256,512]{1,0:T(8,128)(2,1)} %param.24) | copy-start | bytes 786436
  114.1 18.5 %copy-start.4 = (f32[2048]{0:T(1024)S(1)}, f32[2048]{0:T(1024)}, u32[]{:S(2)}) copy-start(f32[2048]{0:T(1024)} %param.26) | copy-start | bytes 24580
  122.8 9.9 %collective-permute-start.4 = (bf16[256,512]{1,0:T(8,128)(2,1)S(1)}, bf16[256,512]{1,0:T(8,128)(2,1)S(1)}, u32[]{:S(2)}, u32[]{:S(2)}) collective-permute-start(bf16[256,512]{1,0:T(8,128)(2,1)S(1)} %fusion.26), channel_id=1, source_target_pairs={{0,1},{1,2},{2,3},{3,0},{4,5},{5,6},{6,7},{7,4},{8,9},{9,10},{10,1... | collective-permute-start | bytes 786440 | tf_op jit(solution)/shard_map/ppermute | solution.py:75
  125.9 10.6 %collective-permute-start.5 = (bf16[256,512]{1,0:T(8,128)(2,1)S(1)}, bf16[256,512]{1,0:T(8,128)(2,1)S(1)}, u32[]{:S(2)}, u32[]{:S(2)}) collective-permute-start(bf16[256,512]{1,0:T(8,128)(2,1)S(1)} %fusion.26), channel_id=1, source_target_pairs={{0,2},{1,3},{2,0},{3,1},{4,6},{5,7},{6,4},{7,5},{8,10},{9,11},{10,... | collective-permute-start | bytes 786440 | tf_op jit(solution)/shard_map/ppermute | solution.py:75
  128.5 14.7 %collective-permute-start.6 = (bf16[256,512]{1,0:T(8,128)(2,1)S(1)}, bf16[256,512]{1,0:T(8,128)(2,1)S(1)}, u32[]{:S(2)}, u32[]{:S(2)}) collective-permute-start(bf16[256,512]{1,0:T(8,128)(2,1)S(1)} %fusion.26), channel_id=1, source_target_pairs={{0,3},{1,0},{2,1},{3,2},{4,7},{5,4},{6,5},{7,6},{8,11},{9,8},{10,9... | collective-permute-start | bytes 786440 | tf_op jit(solution)/shard_map/ppermute | solution.py:75
  154.2 0.8 copy-start.3
  160.6 10.1 %collective-permute-start.7 = (bf16[256,512]{1,0:T(8,128)(2,1)}, bf16[256,512]{1,0:T(8,128)(2,1)}, u32[]{:S(2)}, u32[]{:S(2)}) collective-permute-start(bf16[256,512]{1,0:T(8,128)(2,1)} %copy.63), channel_id=1, source_target_pairs={{0,1},{1,2},{2,3},{3,0},{4,5},{5,6},{6,7},{7,4},{8,9},{9,10},{10,1... | collective-permute-start | bytes 786440 | tf_op jit(solution)/shard_map/ppermute | solution.py:105
  163.4 10.3 %collective-permute-start.8 = (bf16[256,512]{1,0:T(8,128)(2,1)}, bf16[256,512]{1,0:T(8,128)(2,1)S(1)}, u32[]{:S(2)}, u32[]{:S(2)}) collective-permute-start(bf16[256,512]{1,0:T(8,128)(2,1)} %copy.65), channel_id=1, source_target_pairs={{0,2},{1,3},{2,0},{3,1},{4,6},{5,7},{6,4},{7,5},{8,10},{9,11},{10,... | collective-permute-start | bytes 786440 | tf_op jit(solution)/shard_map/ppermute | solution.py:105
  166.4 14.4 %collective-permute-start.9 = (bf16[256,512]{1,0:T(8,128)(2,1)}, bf16[256,512]{1,0:T(8,128)(2,1)S(1)}, u32[]{:S(2)}, u32[]{:S(2)}) collective-permute-start(bf16[256,512]{1,0:T(8,128)(2,1)} %copy.66), channel_id=1, source_target_pairs={{0,3},{1,0},{2,1},{3,2},{4,7},{5,4},{6,5},{7,6},{8,11},{9,8},{10,9... | collective-permute-start | bytes 786440 | tf_op jit(solution)/shard_map/ppermute | solution.py:105
Sparse Core Ops, SparseCore 0:
  17.4 86.6 all-gather.1
where the time goes:
time: 190 us
  waiting for transfers between devices  72.5 us (38%)
  starting transfers between devices  35.2 us (19%)
  matrix products  24.2 us (13%)
  local copies, waits for them, and re-layouts  18.8 us (10%)
  between operations  15.9 us (8%)
  other arithmetic  13 us (7%)
  blocking collectives  9.79 us (5%)
    all_gather x1, waiting for transfers between devices, gather_over_xz(): return lax.all_gather(out, 'z', axis=0, tiled=True)  39.7 us
    ppermute x6, starting transfers between devices, mlp_gather(): lax.ppermute(block, 'mlp', [(i, (i + shift) % axis_size) for i in range(a...  19.5 us
    ppermute x6, waiting for transfers between devices, mlp_gather(): lax.ppermute(block, 'mlp', [(i, (i + shift) % axis_size) for i in range(a...  15.6 us
    ppermute x3, waiting for transfers between devices, down_and_scatter(): lax.ppermute(block_for(target), 'mlp', [(i, (i + shift) % axis_size) for...  10.2 us
    all_gather x1, blocking collectives, gather_over_xz(): out = lax.all_gather(block, 'x', axis=0, tiled=True)  9.79 us
    dot_general x4, matrix products, split_dot(): jnp.dot(act[:, j * size:(j + 1) * size], half, preferred_element_type=jnp...  9.13 us
    ppermute x3, starting transfers between devices, down_and_scatter(): lax.ppermute(block_for(target), 'mlp', [(i, (i + shift) % axis_size) for...  8.04 us
    ppermute x1, starting transfers between devices, swap_with_core(): return [rows_xz, lax.ppermute(rows_xz, 'c', [(0, 1), (1, 0)])]  7.73 us
  transfers between devices with their start and end apart: 11, of which 8 were waited for; matrix products, arithmetic and copies ran while one was open for 18% of the time, Pallas kernels for 0%

commit v1 on v0

--- a/solution.py
+++ b/solution.py
@@ -6,6 +6,13 @@
 D = 2048
 NEG_FILL = -1e30
 LAMBDA_BASE = 0.2
+
+
+def meet_chunk(original):
+    block_last = jnp.concatenate(
+        lax.all_to_all(jnp.stack([original] * lax.axis_size("x"), axis=0), "x", 0, 0), axis=0
+    )
+    return block_last
 
 
 def attend(
@@ -116,7 +123,7 @@
 
 
 def gather_over_xz(block):
-    out = lax.all_gather(block, "x", axis=0, tiled=True)
+    out = meet_chunk(block)
     return lax.all_gather(out, "z", axis=0, tiled=True)
 
 

time: 190 us -> 187 us (0.984)
  the two profiles are of different devices: /device:TPU:13 before, /device:TPU:15 now
where the time goes in v1:
time: 187 us; the launch traced here: 186 us
  waiting for transfers between devices  69.9 us (37%)
  starting transfers between devices  35.3 us (19%)
  matrix products  24.1 us (13%)
  local copies, waits for them, and re-layouts  18.8 us (10%)
  between operations  15.9 us (9%)
  other arithmetic  13 us (7%)
  blocking collectives  9.14 us (5%)
    all_gather x1, waiting for transfers between devices, gather_over_xz(): return lax.all_gather(out, 'z', axis=0, tiled=True)  35.2 us
    ppermute x6, starting transfers between devices, mlp_gather(): lax.ppermute(block, 'mlp', [(i, (i + shift) % axis_size) for i in range(a...  19.2 us
    ppermute x6, waiting for transfers between devices, mlp_gather(): lax.ppermute(block, 'mlp', [(i, (i + shift) % axis_size) for i in range(a...  17.8 us
    ppermute x3, waiting for transfers between devices, down_and_scatter(): lax.ppermute(block_for(target), 'mlp', [(i, (i + shift) % axis_size) for...  9.85 us
    all_to_all x1, blocking collectives, meet_chunk(): lax.all_to_all(jnp.stack([original] * lax.axis_size('x'), axis=0), 'x', 0...  9.14 us
    dot_general x4, matrix products, split_dot(): jnp.dot(act[:, j * size:(j + 1) * size], half, preferred_element_type=jnp...  9.13 us
    ppermute x3, starting transfers between devices, down_and_scatter(): lax.ppermute(block_for(target), 'mlp', [(i, (i + shift) % axis_size) for...  8.36 us
    ppermute x1, starting transfers between devices, swap_with_core(): return [rows_xz, lax.ppermute(rows_xz, 'c', [(0, 1), (1, 0)])]  7.73 us
  transfers between devices with their start and end apart: 11, of which 8 were waited for; matrix products, arithmetic and copies ran while one was open for 18% of the time, Pallas kernels for 0%

profile of v1, /device:TPU:15, one launch (start us, length us, event | category | flops | bytes accessed | tf_op | source)
XLA Modules:
  0.0 186.3 jit_solution(17714329373888779499)
XLA Ops:
  6.5 0.9 pad_maximum_fusion.19
  7.5 9.1 %all_to_all.5 = bf16[4,16,2816]{2,1,0:T(8,128)(2,1)} all-to-all(bf16[4,16,2816]{2,1,0:T(8,128)(2,1)S(1)} %stack.54), channel_id=1, replica_groups=mesh['x'=4,'z'=16,'c'=2,'mlp'=4] {'x'}, dimensions={0} | all-to-all | bytes 720896 | tf_op jit(solution)/shard_map/all_to_all | solution.py:13
  17.3 5.6 %gather_fusion = bf16[6,128,2,512]{3,2,1,0:T(2,128)(2,1)} fusion(bf16[6,128,2,512]{3,2,1,0:T(2,128)(2,1)S(1)} %copy-done, s32[1024]{0:T(1024)S(1)} %pad_clamp_fusion.1), kind=kCustom, calls=%fused_computation.2 | custom fusion | bytes 3145752 | tf_op jit(solution)/shard_map/jit(_take)/gather | solution.py:28
  22.9 1.7 copy.47
  24.7 0.8 copy.48
  26.2 0.7 multiply_reduce_fusion.2
  28.2 0.7 fusion.79
  28.9 0.7 iota_compare_fusion.1
  30.0 1.8 fusion.110
  31.8 1.5 bitcast_select_fusion.4
  33.3 2.3 %fusion.111 = f32[256,2]{0,1:T(2,128)S(1)} fusion(pred[256,1024]{0,1:T(8,128)(4,1)S(1)} %pad_add_fusion, bf16[768,2,512]{2,0,1:T(8,128)(2,1)} %bitcast_select_fusion.4, bf16[256,2,512]{2,0,1:T(8,128)(2,1)} %copy.48, bf16[256,2,128]{2,1,0:T(2,128)(2,1)} %get-tuple-element.33), kind=kOutput, calls=%fused_computation.142 | convolution fusion | flops 137888768 | bytes 2754560 | tf_op jit(solution)/shard_map/sub | solution.py:50
  35.5 3.2 %fusion.21 = f32[256,2,256]{0,2,1:T(8,128)} fusion(f32[256,2]{0,1:T(2,128)S(1)} %fusion.111, pred[256,1024]{0,1:T(8,128)(4,1)S(1)} %pad_add_fusion, bf16[768,2,512]{2,0,1:T(8,128)(2,1)S(1)} %copy-done.1, bf16[256,2,512]{2,0,1:T(8,128)(2,1)} %copy.48, bf16[256,2,128]{2,1,0:T(2,128)(2,1)} %get-tuple-element.33), kind=kOutput, calls=%fused_computation.34 | convolution fusion | flops 408552960 | bytes 5376000 | tf_op jit(solution)/shard_map/nhk,khd->nhd/dot_general | solution.py:52
  38.8 2.0 %fusion.116 = f32[256,2]{0,1:T(2,128)S(1)} fusion(pred[256,1024]{0,1:T(8,128)(4,1)S(1)} %pad_add_fusion, bf16[256,2,512]{2,0,1:T(8,128)(2,1)} %copy.48, bf16[768,2,512]{2,0,1:T(8,128)(2,1)S(1)} %copy-done.1, bf16[256,2,128]{2,1,0:T(2,128)(2,1)S(1)} %get-tuple-element.32), kind=kOutput, calls=%fused_computation.143 | convolution fusion | flops 137888768 | bytes 2492416 | tf_op jit(solution)/shard_map/sub | solution.py:50
  40.8 3.4 %multiply_reduce_fusion.1 = (f32[256,2]{0,1:T(2,128)S(1)}, f32[256,2,256]{0,2,1:T(8,128)}) fusion(f32[256,2,256]{0,2,1:T(8,128)} %fusion.21, f32[256,2]{0,1:T(2,128)S(1)} %fusion.116, pred[256,1024]{0,1:T(8,128)(4,1)S(1)} %pad_add_fusion, bf16[256,2,512]{2,0,1:T(8,128)(2,1)} %copy.48, bf16[768,2,512]{2,0,1:T(8,128)(2,1)S(1)} %copy-done.1, ...), kind=kOutput, calls=%fused_computation.73 | convolution fusion | flops 409076736 | bytes 5902340 | tf_op jit(solution)/shard_map/nhk,khd->nhd/dot_general | solution.py:52
  44.1 1.2 multiply_convert_fusion.1
  45.3 3.2 %collective-permute-start = (bf16[256,512]{0,1:T(8,128)(2,1)S(1)}, bf16[256,512]{0,1:T(8,128)(2,1)S(1)}, u32[]{:S(2)}, u32[]{:S(2)}) collective-permute-start(bf16[256,512]{0,1:T(8,128)(2,1)S(1)} %bitcast.107), channel_id=1, source_target_pairs={{0,1},{1,2},{2,3},{3,0},{4,5},{5,6},{6,7},{7,4},{8,9},{9,10},{10,1... | collective-permute-start | bytes 786440 | tf_op jit(solution)/shard_map/ppermute | solution.py:82
  48.5 2.6 %collective-permute-start.1 = (bf16[256,512]{0,1:T(8,128)(2,1)S(1)}, bf16[256,512]{0,1:T(8,128)(2,1)S(1)}, u32[]{:S(2)}, u32[]{:S(2)}) collective-permute-start(bf16[256,512]{0,1:T(8,128)(2,1)S(1)} %bitcast.108), channel_id=1, source_target_pairs={{0,2},{1,3},{2,0},{3,1},{4,6},{5,7},{6,4},{7,5},{8,10},{9,11},{10,... | collective-permute-start | bytes 786440 | tf_op jit(solution)/shard_map/ppermute | solution.py:82
  51.2 4.0 %collective-permute-start.2 = (bf16[256,512]{0,1:T(8,128)(2,1)S(1)}, bf16[256,512]{0,1:T(8,128)(2,1)S(1)}, u32[]{:S(2)}, u32[]{:S(2)}) collective-permute-start(bf16[256,512]{0,1:T(8,128)(2,1)S(1)} %bitcast.109), channel_id=1, source_target_pairs={{0,3},{1,0},{2,1},{3,2},{4,7},{5,4},{6,5},{7,6},{8,11},{9,8},{10,9... | collective-permute-start | bytes 786440 | tf_op jit(solution)/shard_map/ppermute | solution.py:82
  55.2 2.4 %collective-permute-done.1 = bf16[256,512]{0,1:T(8,128)(2,1)S(1)} collective-permute-done((bf16[256,512]{0,1:T(8,128)(2,1)S(1)}, bf16[256,512]{0,1:T(8,128)(2,1)S(1)}, u32[]{:S(2)}, u32[]{:S(2)}) %collective-permute-start.1) | collective-permute-done | bytes 262176 | tf_op jit(solution)/shard_map/ppermute | solution.py:82
  57.6 4.6 %collective-permute-done.2 = bf16[256,512]{0,1:T(8,128)(2,1)S(1)} collective-permute-done((bf16[256,512]{0,1:T(8,128)(2,1)S(1)}, bf16[256,512]{0,1:T(8,128)(2,1)S(1)}, u32[]{:S(2)}, u32[]{:S(2)}) %collective-permute-start.2) | collective-permute-done | bytes 262176 | tf_op jit(solution)/shard_map/ppermute | solution.py:82
  62.1 1.1 pad_maximum_fusion
  63.3 1.9 gather_fusion.1
  65.5 35.2 %all-gather.2.cloned.1.call-done = bf16[1024,2816]{1,0:T(8,128)(2,1)} async-done(((bf16[64,2816]{1,0:T(8,128)(2,1)}), bf16[1024,2816]{1,0:T(8,128)(2,1)}) %all-gather.2.cloned.1.call-update) | async-done | bytes 5767184 | tf_op jit(solution)/shard_map/all_gather | solution.py:127
  100.7 7.7 %collective-permute-start.3 = (bf16[1024,2816]{1,0:T(8,128)(2,1)}, bf16[1024,2816]{1,0:T(8,128)(2,1)}, u32[]{:S(2)}, u32[]{:S(2)}) collective-permute-start(bf16[1024,2816]{1,0:T(8,128)(2,1)} %all-gather.2.cloned.1.call-done), channel_id=1, source_target_pairs={{0,4},{4,0},{1,5},{5,1},{2,6},{6,2},{3,7},{7,3},{8,12},{12,8},{9,1... | collective-permute-start | bytes 17301512 | tf_op jit(solution)/shard_map/ppermute | solution.py:131
  109.0 1.7 fusion.31
  110.7 7.0 %collective-permute-done.3 = bf16[1024,2816]{1,0:T(8,128)(2,1)} collective-permute-done((bf16[1024,2816]{1,0:T(8,128)(2,1)}, bf16[1024,2816]{1,0:T(8,128)(2,1)}, u32[]{:S(2)}, u32[]{:S(2)}) %collective-permute-start.3) | collective-permute-done | bytes 5767200 | tf_op jit(solution)/shard_map/ppermute | solution.py:131
  117.8 1.7 fusion.26
  119.4 3.2 %collective-permute-start.4 = (bf16[256,512]{1,0:T(8,128)(2,1)S(1)}, bf16[256,512]{1,0:T(8,128)(2,1)S(1)}, u32[]{:S(2)}, u32[]{:S(2)}) collective-permute-start(bf16[256,512]{1,0:T(8,128)(2,1)S(1)} %fusion.26), channel_id=1, source_target_pairs={{0,1},{1,2},{2,3},{3,0},{4,5},{5,6},{6,7},{7,4},{8,9},{9,10},{10,1... | collective-permute-start | bytes 786440 | tf_op jit(solution)/shard_map/ppermute | solution.py:82
  122.7 2.7 %collective-permute-start.5 = (bf16[256,512]{1,0:T(8,128)(2,1)S(1)}, bf16[256,512]{1,0:T(8,128)(2,1)S(1)}, u32[]{:S(2)}, u32[]{:S(2)}) collective-permute-start(bf16[256,512]{1,0:T(8,128)(2,1)S(1)} %fusion.26), channel_id=1, source_target_pairs={{0,2},{1,3},{2,0},{3,1},{4,6},{5,7},{6,4},{7,5},{8,10},{9,11},{10,... | collective-permute-start | bytes 786440 | tf_op jit(solution)/shard_map/ppermute | solution.py:82
  125.4 3.4 %collective-permute-start.6 = (bf16[256,512]{1,0:T(8,128)(2,1)S(1)}, bf16[256,512]{1,0:T(8,128)(2,1)S(1)}, u32[]{:S(2)}, u32[]{:S(2)}) collective-permute-start(bf16[256,512]{1,0:T(8,128)(2,1)S(1)} %fusion.26), channel_id=1, source_target_pairs={{0,3},{1,0},{2,1},{3,2},{4,7},{5,4},{6,5},{7,6},{8,11},{9,8},{10,9... | collective-permute-start | bytes 786440 | tf_op jit(solution)/shard_map/ppermute | solution.py:82
  129.1 4.2 %collective-permute-done.5 = bf16[256,512]{1,0:T(8,128)(2,1)S(1)} collective-permute-done((bf16[256,512]{1,0:T(8,128)(2,1)S(1)}, bf16[256,512]{1,0:T(8,128)(2,1)S(1)}, u32[]{:S(2)}, u32[]{:S(2)}) %collective-permute-start.5) | collective-permute-done | bytes 262176 | tf_op jit(solution)/shard_map/ppermute | solution.py:82
  133.3 6.6 %collective-permute-done.6 = bf16[256,512]{1,0:T(8,128)(2,1)S(1)} collective-permute-done((bf16[256,512]{1,0:T(8,128)(2,1)S(1)}, bf16[256,512]{1,0:T(8,128)(2,1)S(1)}, u32[]{:S(2)}, u32[]{:S(2)}) %collective-permute-start.6) | collective-permute-done | bytes 262176 | tf_op jit(solution)/shard_map/ppermute | solution.py:82
  139.9 1.1 pad_maximum_fusion.2
  141.0 1.8 gather_fusion.2
  145.0 2.9 %fusion.4 = f32[256,1536]{1,0:T(8,128)S(1)} fusion(bf16[1024,2816]{1,0:T(8,128)(2,1)} %all-gather.2.cloned.1.call-done, bf16[256,2048]{0,1:T(8,128)(2,1)S(1)} %bitcast.96), kind=kOutput, calls=%fused_computation.7 | convolution fusion | flops 805306368 | bytes 5242880 | tf_op jit(solution)/shard_map/dot_general | solution.py:138
  147.9 2.9 %fusion.6 = f32[256,1536]{1,0:T(8,128)S(1)} fusion(f32[256,1536]{1,0:T(8,128)S(1)} %fusion.4, bf16[1024,2816]{1,0:T(8,128)(2,1)} %collective-permute-done.3, bf16[256,2048]{0,1:T(8,128)(2,1)S(1)} %bitcast.97), kind=kOutput, calls=%fused_computation.9 | convolution fusion | flops 805699584 | bytes 6815744 | tf_op jit(solution)/shard_map/dot_general | solution.py:138
  151.0 0.7 copy-done.3
  151.8 2.0 %fusion.15 = bf16[256,1024]{1,0:T(8,128)(2,1)S(1)} fusion(bf16[256,768]{1,0:T(8,128)(2,1)S(1)} %fusion.41, bf16[1024,2816]{1,0:T(8,128)(2,1)} %all-gather.2.cloned.1.call-done), kind=kOutput, calls=%fused_computation.29 | convolution fusion | flops 402915328 | bytes 2490368 | tf_op jit(solution)/shard_map/dot_general | solution.py:97
  154.0 2.1 %fusion.18 = bf16[256,1024]{1,0:T(8,128)(2,1)S(1)} fusion(bf16[256,768]{1,0:T(8,128)(2,1)} %copy-done.3, bf16[1024,2816]{1,0:T(8,128)(2,1)} %collective-permute-done.3), kind=kOutput, calls=%fused_computation.30 | convolution fusion | flops 402915328 | bytes 2490368 | tf_op jit(solution)/shard_map/dot_general | solution.py:97
  156.5 0.8 copy.63
  157.4 1.9 %collective-permute-start.7 = (bf16[256,512]{1,0:T(8,128)(2,1)}, bf16[256,512]{1,0:T(8,128)(2,1)}, u32[]{:S(2)}, u32[]{:S(2)}) collective-permute-start(bf16[256,512]{1,0:T(8,128)(2,1)} %copy.63), channel_id=1, source_target_pairs={{0,1},{1,2},{2,3},{3,0},{4,5},{5,6},{6,7},{7,4},{8,9},{9,10},{10,1... | collective-permute-start | bytes 786440 | tf_op jit(solution)/shard_map/ppermute | solution.py:112
  159.3 0.8 copy.65
  160.2 2.5 %collective-permute-start.8 = (bf16[256,512]{1,0:T(8,128)(2,1)}, bf16[256,512]{1,0:T(8,128)(2,1)S(1)}, u32[]{:S(2)}, u32[]{:S(2)}) collective-permute-start(bf16[256,512]{1,0:T(8,128)(2,1)} %copy.65), channel_id=1, source_target_pairs={{0,2},{1,3},{2,0},{3,1},{4,6},{5,7},{6,4},{7,5},{8,10},{9,11},{10,... | collective-permute-start | bytes 786440 | tf_op jit(solution)/shard_map/ppermute | solution.py:112
  162.7 0.8 copy.66
  163.5 4.0 %collective-permute-start.9 = (bf16[256,512]{1,0:T(8,128)(2,1)}, bf16[256,512]{1,0:T(8,128)(2,1)S(1)}, u32[]{:S(2)}, u32[]{:S(2)}) collective-permute-start(bf16[256,512]{1,0:T(8,128)(2,1)} %copy.66), channel_id=1, source_target_pairs={{0,3},{1,0},{2,1},{3,2},{4,7},{5,4},{6,5},{7,6},{8,11},{9,8},{10,9... | collective-permute-start | bytes 786440 | tf_op jit(solution)/shard_map/ppermute | solution.py:112
  167.8 2.7 %collective-permute-done.8 = bf16[256,512]{1,0:T(8,128)(2,1)S(1)} collective-permute-done((bf16[256,512]{1,0:T(8,128)(2,1)}, bf16[256,512]{1,0:T(8,128)(2,1)S(1)}, u32[]{:S(2)}, u32[]{:S(2)}) %collective-permute-start.8) | collective-permute-done | bytes 262176 | tf_op jit(solution)/shard_map/ppermute | solution.py:112
  170.5 7.1 %collective-permute-done.9 = bf16[256,512]{1,0:T(8,128)(2,1)S(1)} collective-permute-done((bf16[256,512]{1,0:T(8,128)(2,1)}, bf16[256,512]{1,0:T(8,128)(2,1)S(1)}, u32[]{:S(2)}, u32[]{:S(2)}) %collective-permute-start.9) | collective-permute-done | bytes 262176 | tf_op jit(solution)/shard_map/ppermute | solution.py:112
  177.6 1.8 add_convert_fusion
  (61 shorter events, 5.3 us)
Async XLA Ops:
  6.5 10.8 %copy-start = (bf16[6,128,2,512]{3,2,1,0:T(2,128)(2,1)S(1)}, bf16[6,128,2,512]{3,2,1,0:T(2,128)(2,1)}, u32[]{:S(2)}) copy-start(bf16[6,128,2,512]{3,2,1,0:T(2,128)(2,1)} %param.18) | copy-start | bytes 4718596
  6.5 94.1 %all-gather.2.cloned.1.call-start = ((), (), s32[]{:S(2)}) async-start(), calls=%async_computation.1 | async-start | bytes 6127616 | tf_op jit(solution)/shard_map/all_gather | solution.py:127
  22.9 1.8 copy-start.2
  22.9 3.3 %copy-start.5 = (f32[4,128]{1,0:T(4,128)S(1)}, f32[4,128]{1,0:T(4,128)}, u32[]{:S(2)}) copy-start(f32[4,128]{1,0:T(4,128)} %param.22) | copy-start | bytes 6148
  22.9 5.3 %copy-start.8 = (s32[128]{0:T(128)S(1)}, s32[128]{0:T(128)}, u32[]{:S(2)}) copy-start(s32[128]{0:T(128)} %param.21) | copy-start | bytes 1540
  22.9 6.8 %copy-start.9 = (s32[1,6]{1,0:T(1,128)S(1)}, s32[1,6]{1,0:T(1,128)}, u32[]{:S(2)}) copy-start(s32[1,6]{1,0:T(1,128)} %param.19) | copy-start | bytes 76
  33.3 2.3 %copy-start.1 = (bf16[768,2,512]{2,0,1:T(8,128)(2,1)S(1)}, bf16[768,2,512]{2,0,1:T(8,128)(2,1)}, u32[]{:S(2)}) copy-start(bf16[768,2,512]{2,0,1:T(8,128)(2,1)} %bitcast_select_fusion.4) | copy-start | bytes 4718596
  40.8 3.4 %copy-start.6 = (f32[256]{0:T(256)S(1)}, f32[256]{0:T(256)}, u32[]{:S(2)}) copy-start(f32[256]{0:T(256)} %param.23) | copy-start | bytes 3076
  45.3 9.9 %collective-permute-start = (bf16[256,512]{0,1:T(8,128)(2,1)S(1)}, bf16[256,512]{0,1:T(8,128)(2,1)S(1)}, u32[]{:S(2)}, u32[]{:S(2)}) collective-permute-start(bf16[256,512]{0,1:T(8,128)(2,1)S(1)} %bitcast.107), channel_id=1, source_target_pairs={{0,1},{1,2},{2,3},{3,0},{4,5},{5,6},{6,7},{7,4},{8,9},{9,10},{10,1... | collective-permute-start | bytes 786440 | tf_op jit(solution)/shard_map/ppermute | solution.py:82
  48.5 9.0 %collective-permute-start.1 = (bf16[256,512]{0,1:T(8,128)(2,1)S(1)}, bf16[256,512]{0,1:T(8,128)(2,1)S(1)}, u32[]{:S(2)}, u32[]{:S(2)}) collective-permute-start(bf16[256,512]{0,1:T(8,128)(2,1)S(1)} %bitcast.108), channel_id=1, source_target_pairs={{0,2},{1,3},{2,0},{3,1},{4,6},{5,7},{6,4},{7,5},{8,10},{9,11},{10,... | collective-permute-start | bytes 786440 | tf_op jit(solution)/shard_map/ppermute | solution.py:82
  51.2 11.0 %collective-permute-start.2 = (bf16[256,512]{0,1:T(8,128)(2,1)S(1)}, bf16[256,512]{0,1:T(8,128)(2,1)S(1)}, u32[]{:S(2)}, u32[]{:S(2)}) collective-permute-start(bf16[256,512]{0,1:T(8,128)(2,1)S(1)} %bitcast.109), channel_id=1, source_target_pairs={{0,3},{1,0},{2,1},{3,2},{4,7},{5,4},{6,5},{7,6},{8,11},{9,8},{10,9... | collective-permute-start | bytes 786440 | tf_op jit(solution)/shard_map/ppermute | solution.py:82
  100.7 17.1 %collective-permute-start.3 = (bf16[1024,2816]{1,0:T(8,128)(2,1)}, bf16[1024,2816]{1,0:T(8,128)(2,1)}, u32[]{:S(2)}, u32[]{:S(2)}) collective-permute-start(bf16[1024,2816]{1,0:T(8,128)(2,1)} %all-gather.2.cloned.1.call-done), channel_id=1, source_target_pairs={{0,4},{4,0},{1,5},{5,1},{2,6},{6,2},{3,7},{7,3},{8,12},{12,8},{9,1... | collective-permute-start | bytes 17301512 | tf_op jit(solution)/shard_map/ppermute | solution.py:131
  108.9 8.9 %copy-start.7 = (bf16[256,512]{1,0:T(8,128)(2,1)S(1)}, bf16[256,512]{1,0:T(8,128)(2,1)}, u32[]{:S(2)}) copy-start(bf16[256,512]{1,0:T(8,128)(2,1)} %param.24) | copy-start | bytes 786436
  110.7 18.2 %copy-start.4 = (f32[2048]{0:T(1024)S(1)}, f32[2048]{0:T(1024)}, u32[]{:S(2)}) copy-start(f32[2048]{0:T(1024)} %param.26) | copy-start | bytes 24580
  119.4 9.6 %collective-permute-start.4 = (bf16[256,512]{1,0:T(8,128)(2,1)S(1)}, bf16[256,512]{1,0:T(8,128)(2,1)S(1)}, u32[]{:S(2)}, u32[]{:S(2)}) collective-permute-start(bf16[256,512]{1,0:T(8,128)(2,1)S(1)} %fusion.26), channel_id=1, source_target_pairs={{0,1},{1,2},{2,3},{3,0},{4,5},{5,6},{6,7},{7,4},{8,9},{9,10},{10,1... | collective-permute-start | bytes 786440 | tf_op jit(solution)/shard_map/ppermute | solution.py:82
  122.7 10.6 %collective-permute-start.5 = (bf16[256,512]{1,0:T(8,128)(2,1)S(1)}, bf16[256,512]{1,0:T(8,128)(2,1)S(1)}, u32[]{:S(2)}, u32[]{:S(2)}) collective-permute-start(bf16[256,512]{1,0:T(8,128)(2,1)S(1)} %fusion.26), channel_id=1, source_target_pairs={{0,2},{1,3},{2,0},{3,1},{4,6},{5,7},{6,4},{7,5},{8,10},{9,11},{10,... | collective-permute-start | bytes 786440 | tf_op jit(solution)/shard_map/ppermute | solution.py:82
  125.4 14.5 %collective-permute-start.6 = (bf16[256,512]{1,0:T(8,128)(2,1)S(1)}, bf16[256,512]{1,0:T(8,128)(2,1)S(1)}, u32[]{:S(2)}, u32[]{:S(2)}) collective-permute-start(bf16[256,512]{1,0:T(8,128)(2,1)S(1)} %fusion.26), channel_id=1, source_target_pairs={{0,3},{1,0},{2,1},{3,2},{4,7},{5,4},{6,5},{7,6},{8,11},{9,8},{10,9... | collective-permute-start | bytes 786440 | tf_op jit(solution)/shard_map/ppermute | solution.py:82
  151.0 0.8 copy-start.3
  157.4 10.4 %collective-permute-start.7 = (bf16[256,512]{1,0:T(8,128)(2,1)}, bf16[256,512]{1,0:T(8,128)(2,1)}, u32[]{:S(2)}, u32[]{:S(2)}) collective-permute-start(bf16[256,512]{1,0:T(8,128)(2,1)} %copy.63), channel_id=1, source_target_pairs={{0,1},{1,2},{2,3},{3,0},{4,5},{5,6},{6,7},{7,4},{8,9},{9,10},{10,1... | collective-permute-start | bytes 786440 | tf_op jit(solution)/shard_map/ppermute | solution.py:112
  160.2 10.3 %collective-permute-start.8 = (bf16[256,512]{1,0:T(8,128)(2,1)}, bf16[256,512]{1,0:T(8,128)(2,1)S(1)}, u32[]{:S(2)}, u32[]{:S(2)}) collective-permute-start(bf16[256,512]{1,0:T(8,128)(2,1)} %copy.65), channel_id=1, source_target_pairs={{0,2},{1,3},{2,0},{3,1},{4,6},{5,7},{6,4},{7,5},{8,10},{9,11},{10,... | collective-permute-start | bytes 786440 | tf_op jit(solution)/shard_map/ppermute | solution.py:112
  163.5 14.1 %collective-permute-start.9 = (bf16[256,512]{1,0:T(8,128)(2,1)}, bf16[256,512]{1,0:T(8,128)(2,1)S(1)}, u32[]{:S(2)}, u32[]{:S(2)}) collective-permute-start(bf16[256,512]{1,0:T(8,128)(2,1)} %copy.66), channel_id=1, source_target_pairs={{0,3},{1,0},{2,1},{3,2},{4,7},{5,4},{6,5},{7,6},{8,11},{9,8},{10,9... | collective-permute-start | bytes 786440 | tf_op jit(solution)/shard_map/ppermute | solution.py:112
Sparse Core Ops, SparseCore 0:
  16.8 83.8 all-gather.1
